TPU v7x, 32 devices: a whole 2x2x4 slice. The times are simulated.
32 devices in a mesh: seq: 16 (over z, x, core), head: 2 (over y).
Axes of the slice: x: 2, y: 2, z: 4, core: 2. Of those that a mesh axis runs over, the one named last changes fastest.
Arguments:
- step_tokens: bfloat16 [2, 12, 8, 2560], P(None, None, None, 'head'), may hold values from -6 to 6
- parents: int32 [2, 12, 8], replicated, may hold values from 0 to 7
- tail_cache: bfloat16 [12, 8, 64, 2048], P(None, 'head', 'seq'), may hold values from -192 to 192
- tail_len: int32 [12], replicated, may hold values from 0 to 62, as said below
- cache: bfloat16 [8, 2048, 2048], P(None, ('seq', 'head')), may hold values from -192 to 192
- cache_len: int32 [8], replicated, may hold values from 256 to 2048, as said below
- prompt_states: bfloat16 [4, 128, 2560], P(None, 'seq', 'head'), may hold values from -6 to 6
- prompt_len: int32 [4], replicated, may hold values from 32 to 128, as said below
- in_gain: float32 [2560], P('head'), may hold values from 0.5 to 1.5
- w_query: bfloat16 [2560, 2048], P('head', 'seq'), may hold values from -0.125 to 0.125
- w_keyval: bfloat16 [2560, 2048], P('head', 'seq'), may hold values from -0.125 to 0.125
- q_gain: float32 [256], replicated, may hold values from 0.6 to 32
- k_gain: float32 [256], replicated, may hold values from 0.6 to 32
- w_out: bfloat16 [2048, 2560], P('seq', 'head'), may hold values from -0.125 to 0.125
- post_gain: float32 [2560], P('head'), may hold values from 0.5 to 1.5
- ffn_gain: float32 [2560], P('head'), may hold values from 0.5 to 1.5
- w_gate: bfloat16 [2560, 10240], P('head', 'seq'), may hold values from -0.125 to 0.125
- w_up: bfloat16 [2560, 10240], P('head', 'seq'), may hold values from -0.125 to 0.125
- w_down: bfloat16 [10240, 2560], P('seq', 'head'), may hold values from -0.0625 to 0.0625
- final_gain: float32 [2560], P('head'), may hold values from 0.5 to 1.5
Outputs:
- decoded: bfloat16 [2, 12, 8, 2560], P(None, None, None, 'head')
Inputs may be any that keep to these rules, and one draw needn't show every extreme that they name: `tail_len`: the first 4 groups have 0; the largest entry is exactly 62. `cache_len`: the largest entry is exactly 2048. `prompt_len`: the largest entry is exactly 128.
All inputs are finite; a program needn't handle non-finite values.
Results may differ from a plain program's by a relative error of at most 0.0055.
The roundings to bfloat16 on the way count: a program that leaves them out, or rounds other values in their place, can miss the bound.
Values may be sent and summed in bfloat16 or wider, within the bound.
No kernel may reach another device: no remote copies, remote signals or barrier semaphores. Data moves between devices by JAX's collectives and lax.ppermute only.
A program may use at most 128 MiB of HBM per device.

v0:
```python
import jax
import jax.numpy as jnp
from jax import lax
from jax.sharding import PartitionSpec as P

D = 2560
QH = 8
KVH = 4
HD = 256
QD = 2048


EPS = 1e-06
NEG = -1e30
QSCALE = 0.0625


def norm_heads(values, gain, scale):
    shaped = values.reshape(values.shape[:-1] + (-1, gain.shape[0]))
    shaped = shaped * lax.rsqrt(jnp.mean(shaped * shaped, -1, keepdims=True) + EPS) * gain * scale
    return shaped.reshape(values.shape)


def finish_keys(pairs, k_gain):
    half = pairs.shape[-1] // 2
    keys = norm_heads(pairs[..., :half], k_gain, 1.0)
    return jnp.concatenate([keys, pairs[..., half:]], -1).astype(jnp.bfloat16)


def split_pairs(pairs):
    half = pairs.shape[-1] // 2
    keys = pairs[..., :half].reshape(pairs.shape[:-1] + (KVH, HD))
    values = pairs[..., half:].reshape(pairs.shape[:-1] + (KVH, HD))
    return (keys, values)


def project_tokens(tokens, in_gain, w_query, w_keyval, q_gain, k_gain):
    flat = tokens.reshape(-1, tokens.shape[-1]).astype(jnp.float32)
    scaled = (flat * in_gain).astype(jnp.bfloat16)
    q_part = jnp.dot(scaled, w_query, preferred_element_type=jnp.float32)
    kv_part = jnp.dot(scaled, w_keyval, preferred_element_type=jnp.float32)
    squares = jnp.sum(flat * flat, -1)
    q_part, kv_part, squares = lax.psum((q_part, kv_part, squares), "head")
    factor = lax.rsqrt(squares / D + EPS)[:, None]
    q_raw = (q_part * factor).astype(jnp.bfloat16)
    kv_raw = (kv_part * factor).astype(jnp.bfloat16)
    q_raw, kv_raw = (
        lax.all_gather(q_raw, "seq", axis=1, tiled=True),
        lax.all_gather(kv_raw, "seq", axis=1, tiled=True),
    )
    queries = norm_heads(q_raw.astype(jnp.float32), q_gain, QSCALE).astype(jnp.bfloat16)
    fresh = finish_keys(kv_raw.astype(jnp.float32), k_gain)
    return (queries, fresh)


def shards(
    step_tokens,
    parents,
    tail_cache,
    tail_len,
    cache,
    cache_len,
    prompt_states,
    prompt_len,
    in_gain,
    w_query,
    w_keyval,
    q_gain,
    k_gain,
    w_out,
    post_gain,
    ffn_gain,
    w_gate,
    w_up,
    w_down,
    final_gain,
):
    f32 = jnp.float32
    bf16 = jnp.bfloat16
    n_head = lax.axis_size("head")
    n_seq = lax.axis_size("seq")
    seq_at = lax.axis_index("seq")
    head_at = lax.axis_index("head")
    flat_at = seq_at * n_head + head_at
    steps, groups, beams, width = step_tokens.shape
    pre = prompt_states.shape[0]
    repeat = QH // KVH
    col_block = QD // n_seq
    block_head = jnp.arange(n_seq) * col_block // HD
    head_pick = (jnp.arange(QH)[:, None] == block_head[None, :]).astype(f32)
    rows = jnp.transpose(prompt_states, (1, 0, 2)).astype(f32)
    prompt_scaled = (rows * in_gain).astype(bf16).reshape(-1, width)
    prompt_squares = jnp.sum(rows * rows, -1).reshape(-1)
    prompt_terms = jnp.dot(
        prompt_scaled,
        lax.all_gather(w_keyval, "seq", axis=1, tiled=True),
        preferred_element_type=f32,
    )
    prompt_sum, prompt_sq = (
        lax.psum_scatter(prompt_terms, "head", scatter_dimension=0, tiled=True),
        lax.psum_scatter(prompt_squares, "head", scatter_dimension=0, tiled=True),
    )
    prompt_pairs = finish_keys(prompt_sum * lax.rsqrt(prompt_sq / D + EPS)[:, None], k_gain)
    prompt_seg = prompt_pairs.shape[0] // pre
    prompt_pairs = jnp.transpose(prompt_pairs.reshape(prompt_seg, pre, -1), (1, 0, 2))
    prompt_keys, prompt_values = split_pairs(prompt_pairs)
    prompt_ok = (flat_at * prompt_seg + jnp.arange(prompt_seg))[None, :] < prompt_len[:, None]
    cache_seg = cache.shape[1]
    cache_keys, cache_values = split_pairs(cache)
    cache_ok = (flat_at * cache_seg + jnp.arange(cache_seg))[None, :] < cache_len[:, None]
    tail_seg = tail_cache.shape[2]
    local_beams = tail_cache.shape[1]
    beam_ids = head_at * local_beams + jnp.arange(local_beams)
    offset = (seq_at * tail_seg + jnp.arange(tail_seg))[None, :] - tail_len[:, None]
    all_beams = jnp.arange(beams)
    every_query, every_fresh = project_tokens(
        step_tokens, in_gain, w_query, w_keyval, q_gain, k_gain
    )
    every_query = every_query.reshape(steps, groups, beams, -1)
    every_fresh = every_fresh.reshape(steps, groups, beams, -1)
    tail_state = tail_cache
    decoded = []
    for step in range(steps):
        query = every_query[step]
        new_pairs = every_fresh[step]
        everyone = lax.all_gather(tail_state, "head", axis=1, tiled=True)
        picks = lax.dynamic_slice_in_dim(parents[step], head_at * local_beams, local_beams, 1)
        tail_state = jnp.take_along_axis(everyone, picks[:, :, None, None], axis=1)
        owner = jnp.broadcast_to(all_beams[None, :, None], (groups, beams, tail_seg))
        mine = lax.dynamic_slice_in_dim(new_pairs, head_at * local_beams, local_beams, 1)
        tail_state = jnp.where((offset == step)[:, None, :, None], mine[:, :, None, :], tail_state)
        tail_ok = (offset <= step)[:, None, None, :] & (
            owner[:, :, None, :] == beam_ids[None, None, :, None]
        )
        shaped = query.reshape(groups, beams, KVH, repeat, HD)
        tail_keys, tail_values = split_pairs(tail_state)
        pre_scores = jnp.einsum(
            "gbkrd,gtkd->gbkrt", shaped[:pre], prompt_keys, preferred_element_type=f32
        )
        dec_scores = jnp.einsum(
            "gbkrd,gtkd->gbkrt", shaped[pre:], cache_keys, preferred_element_type=f32
        )
        tail_scores = jnp.einsum(
            "gbkrd,gctkd->gbkrct", shaped, tail_keys, preferred_element_type=f32
        )
        pre_mask = prompt_ok[:, None, None, None, :]
        dec_mask = cache_ok[:, None, None, None, :]
        tail_mask = tail_ok[:, :, None, None, :, :]
        pre_scores = jnp.where(pre_mask, pre_scores, NEG)
        dec_scores = jnp.where(dec_mask, dec_scores, NEG)
        tail_scores = jnp.where(tail_mask, tail_scores, NEG)
        top = jnp.concatenate([jnp.max(pre_scores, -1), jnp.max(dec_scores, -1)], 0)
        top = jnp.maximum(top, jnp.max(tail_scores, (-2, -1)))
        top = lax.pmax(top, ("seq", "head"))
        pre_weights = jnp.where(pre_mask, jnp.exp(pre_scores - top[:pre, ..., None]), 0.0)
        dec_weights = jnp.where(dec_mask, jnp.exp(dec_scores - top[pre:, ..., None]), 0.0)
        tail_weights = jnp.where(tail_mask, jnp.exp(tail_scores - top[..., None, None]), 0.0)
        total = jnp.concatenate([jnp.sum(pre_weights, -1), jnp.sum(dec_weights, -1)], 0)
        total = total + jnp.sum(tail_weights, (-2, -1))
        weighted = jnp.concatenate(
            [
                jnp.einsum(
                    "gbkrt,gtkd->gbkrd",
                    pre_weights.astype(bf16),
                    prompt_values,
                    preferred_element_type=f32,
                ),
                jnp.einsum(
                    "gbkrt,gtkd->gbkrd",
                    dec_weights.astype(bf16),
                    cache_values,
                    preferred_element_type=f32,
                ),
            ],
            0,
        )
        weighted = weighted + jnp.einsum(
            "gbkrct,gctkd->gbkrd",
            tail_weights.astype(bf16),
            tail_values,
            preferred_element_type=f32,
        )
        weighted = weighted.reshape(groups * beams, -1)
        total = total.reshape(groups * beams, -1)
        spread_total = jnp.sum(total[:, :, None] * head_pick[None, :, :], 1)
        share, own_total = (
            lax.psum_scatter(weighted, "seq", scatter_dimension=1, tiled=True),
            lax.psum_scatter(spread_total, "seq", scatter_dimension=1, tiled=True),
        )
        share, own_total = lax.psum((share, own_total), "head")
        attn = (share / own_total).astype(bf16)
        partial_out = jnp.dot(attn, w_out, preferred_element_type=f32)
        out_proj = lax.psum(partial_out, "seq")
        out_sq = lax.psum(jnp.sum(out_proj * out_proj, -1), "head")
        x_f = step_tokens[step].reshape(groups * beams, -1).astype(f32)
        state = (x_f + out_proj * lax.rsqrt(out_sq / D + EPS)[:, None] * post_gain).astype(bf16)
        state = lax.optimization_barrier(state)
        state_f = state.astype(f32)
        scaled_two = (state_f * ffn_gain).astype(bf16)
        gate_part = jnp.dot(scaled_two, w_gate, preferred_element_type=f32)
        up_part = jnp.dot(scaled_two, w_up, preferred_element_type=f32)
        gate_part, up_part, state_sq = lax.psum(
            (gate_part, up_part, jnp.sum(state_f * state_f, -1)), "head"
        )
        norm_s = lax.rsqrt(state_sq / D + EPS)[:, None]
        inner = (jax.nn.gelu(gate_part * norm_s, approximate=True) * (up_part * norm_s)).astype(
            bf16
        )
        ffn_out = lax.psum(jnp.dot(inner, w_down, preferred_element_type=f32), "seq")
        ffn_sq = lax.psum(jnp.sum(ffn_out * ffn_out, -1), "head")
        result = (state_f + ffn_out * lax.rsqrt(ffn_sq / D + EPS)[:, None] * final_gain).astype(
            bf16
        )
        decoded.append(result.reshape(groups, beams, -1))
    return jnp.stack(decoded)


def solution(mesh):
    return jax.shard_map(
        shards,
        mesh=mesh,
        in_specs=(
            P(None, None, None, "head"),
            P(),
            P(None, "head", "seq", None),
            P(),
            P(None, ("seq", "head"), None),
            P(),
            P(None, "seq", "head"),
            P(),
            P("head"),
            P("head", "seq"),
            P("head", "seq"),
            P(),
            P(),
            P("seq", "head"),
            P("head"),
            P("head"),
            P("head", "seq"),
            P("head", "seq"),
            P("seq", "head"),
            P("head"),
        ),
        out_specs=P(None, None, None, "head"),
        check_vma=False,
    )
```

profile of v0, /device:TPU:0, one launch (start us, length us, event | category | flops | bytes accessed | tf_op | source)
XLA Modules:
  0.0 628.8 jit_solution(9408125753058318404)
XLA Ops:
  6.5 1.3 fusion.9
  7.9 1.9 fusion.145
  12.6 5.8 all-reduce.11
  19.1 17.0 %all-reduce.28.cloned.1.call-done = (f32[192,128]{1,0:T(8,128)}, f32[192,128]{1,0:T(8,128)}) async-done(((f32[192,128]{1,0:T(8,128)}, f32[192,128]{1,0:T(8,128)}), (f32[192,128]{1,0:T(8,128)}, f32[192,128]{1,0:T(8,128)})) %all-reduce.28.cloned.1.call-update) | async-done | bytes 196624 | tf_op jit(solution)/shard_map/psum | solution.py:43
  36.1 1.0 multiply_convert_fusion
  37.1 23.5 %all_gather.17 = bf16[192,2048]{1,0:T(8,128)(2,1)S(1)} all-gather(bf16[192,128]{1,0:T(8,128)(2,1)S(1)} %get-tuple-element.70), channel_id=1, replica_groups=mesh['seq'=16,'head'=2] {'seq'}, dimensions={1}, use_global_device_ids=true | all-gather | bytes 835584 | tf_op jit(solution)/shard_map/all_gather | solution.py:49
  62.4 1.5 mul.381
  66.4 2.9 gather_fusion
  69.4 1.7 select_select_fusion.1
  73.5 2.7 fusion.131
  76.3 1.6 reshape.377
  77.9 1.9 reshape.375
  83.1 22.2 %all_gather.16 = bf16[192,2048]{1,0:T(8,128)(2,1)S(1)} all-gather(bf16[192,128]{1,0:T(8,128)(2,1)S(1)} %get-tuple-element.71), channel_id=1, replica_groups=mesh['seq'=16,'head'=2] {'seq'}, dimensions={1}, use_global_device_ids=true | all-gather | bytes 835584 | tf_op jit(solution)/shard_map/all_gather | solution.py:48
  105.5 1.8 copy.246
  107.2 2.4 reduce_sum.180
  111.3 1.2 mul.367
  114.6 1.7 fusion.139
  116.4 1.7 fusion.141
  121.2 2.0 fusion.37
  124.3 4.0 gather_fusion.1
  128.3 1.9 select_select_fusion
  130.2 28.0 %all-gather.4.cloned.1.call-done = bf16[1280,2048]{1,0:T(8,128)(2,1)} async-done(((bf16[1280,128]{1,0:T(8,128)(2,1)}), bf16[1280,2048]{1,0:T(8,128)(2,1)}) %all-gather.4.cloned.1.call-update) | async-done | bytes 5242896 | tf_op jit(solution)/shard_map/all_gather | solution.py:96
  158.2 4.2 fusion.143
  162.5 1.2 fusion.133
  164.5 2.1 fusion.34
  167.7 4.7 reduce-scatter.4.cloned.1.call-done
  172.4 1.0 broadcast_multiply_fusion
  173.9 1.9 fusion.142
  175.9 1.9 fusion.140
  177.9 40.8 %all-reduce.3 = (f32[12,8,4,2]{1,3,2,0:T(2,128)S(1)}, f32[12,8,4,2]{1,3,2,0:T(2,128)S(1)}) all-reduce(f32[12,8,4,2]{1,3,2,0:T(2,128)S(1)} %maximum_maximum_fusion.1, f32[12,8,4,2]{1,3,2,0:T(2,128)S(1)} %maximum_maximum_fusion), channel_id=1, replica_groups=mesh['seq'=16,'head'=2] {'seq','head'}, use_global_device_ids=true, to_apply=%region_35.37 | all-reduce | flops 1536 | bytes 12288 | tf_op jit(solution)/shard_map/pmax | solution.py:154
  220.0 1.5 fusion.27
  221.5 1.1 copy.192
  222.7 1.2 convolution_bitcast_fusion.5
  223.8 1.6 convolution_bitcast_fusion.3
  225.4 1.4 fusion.4
  227.9 1.1 copy.207
  229.1 1.0 convolution_bitcast_fusion.4
  230.1 1.6 convolution_bitcast_fusion.2
  231.7 1.4 fusion.3
  235.1 60.1 %all-reduce.4 = (f32[96,16]{0,1:T(8,128)S(1)}, f32[96,16]{0,1:T(8,128)S(1)}) all-reduce(f32[96,16]{0,1:T(8,128)S(1)} %get-tuple-element.7, f32[96,16]{0,1:T(8,128)S(1)} %get-tuple-element.6), channel_id=7, replica_groups=mesh['seq'=16,'head'=2] {'seq'}, use_global_device_ids=true, to_apply=%region_42.44.clone | all-reduce | flops 3072 | bytes 24576
  295.2 1.2 fusion.116
  296.4 1.2 fusion.115
  297.6 45.9 %reduce-scatter.8.cloned.1.call-done = f32[96,128]{1,0:T(8,128)} async-done(((f32[96,2048]{1,0:T(8,128)}), f32[96,128]{1,0:T(8,128)}) %reduce-scatter.8.cloned.1.call-update) | async-done | bytes 49168 | tf_op jit(solution)/shard_map/reduce_scatter | solution.py:187
  343.6 22.5 %all-reduce.24.cloned.1.call-done = (f32[96,128]{1,0:T(8,128)}, f32[96]{0:T(128)}, f32[96,128]{1,0:T(8,128)}, f32[96]{0:T(128)}) async-done(((f32[96,128]{1,0:T(8,128)}, f32[96]{0:T(128)}, f32[96,128]{1,0:T(8,128)}, f32[96]{0:T(128)}), (f32[96,128]{1,0:T(8,128)}, f32[96]{0:T(128)}, f32[96,128]{1,0:T(8,128)}, f32[96]{0:T(128)})) %all-reduce.24.cloned.1.call-update) | async-done | bytes 99088 | tf_op jit(solution)/shard_map/psum | solution.py:190
  366.1 1.9 fusion.111
  367.9 1.9 fusion.110
  369.9 94.0 %all-reduce.22.cloned.1.call-done = (f32[96,1280]{1,0:T(8,128)}, f32[96,1280]{1,0:T(8,128)}) async-done(((f32[96,1280]{1,0:T(8,128)}, f32[96,1280]{1,0:T(8,128)}), (f32[96,1280]{1,0:T(8,128)}, f32[96,1280]{1,0:T(8,128)})) %all-reduce.22.cloned.1.call-update) | async-done | bytes 983056 | tf_op jit(solution)/shard_map/psum | solution.py:193
  463.9 1.2 multiply_reduce_fusion.2
  465.0 1.2 multiply_reduce_fusion.4
  466.2 4.9 all-reduce.9
  471.2 1.7 fusion.25
  472.9 1.1 fusion.63
  474.0 1.1 fusion.65
  475.1 1.1 fusion.67
  476.2 1.1 fusion.69
  477.7 4.9 all-reduce.8
  482.7 33.1 %all-reduce.26.cloned.1.call-done = (f32[96,640]{1,0:T(8,128)}, f32[96,640]{1,0:T(8,128)}, f32[96,640]{1,0:T(8,128)}, f32[96,640]{1,0:T(8,128)}) async-done(((f32[96,640]{1,0:T(8,128)}, f32[96,640]{1,0:T(8,128)}, f32[96,640]{1,0:T(8,128)}, f32[96,640]{1,0:T(8,128)}), (f32[96,640]{1,0:T(8,128)}, f32[96,640]{1,0:T(8,128)}, f32[96,640]{1,0:T(8,128)}, f32[96,640]{1,0:T(8,128)})) %all-reduce.26.cloned.1.call-update) | async-done | bytes 983056 | tf_op jit(solution)/shard_map/psum | solution.py:202
  515.7 2.4 fusion.81
  518.1 1.3 fusion.83
  519.5 93.3 %all-reduce.20.cloned.1.call-done = (f32[96,1280]{1,0:T(8,128)}, f32[96,1280]{1,0:T(8,128)}) async-done(((f32[96,1280]{1,0:T(8,128)}, f32[96,1280]{1,0:T(8,128)}), (f32[96,1280]{1,0:T(8,128)}, f32[96,1280]{1,0:T(8,128)})) %all-reduce.20.cloned.1.call-update) | async-done | bytes 983056 | tf_op jit(solution)/shard_map/psum | solution.py:209
  612.8 1.2 multiply_reduce_fusion.1
  613.9 1.2 multiply_reduce_fusion.3
  615.1 4.9 all-reduce.7
  620.1 1.4 fusion.58
  (242 shorter events, 29.1 us)
Async XLA Ops:
  6.5 509.2 %copy-start = (bf16[640,1280]{1,0:T(8,128)(2,1)S(1)}, bf16[640,1280]{1,0:T(8,128)(2,1)}, u32[]{:S(2)}) copy-start(bf16[640,1280]{1,0:T(8,128)(2,1)} %param.40) | copy-start | bytes 4915204
  6.5 3.3 copy-start.16
  6.5 29.6 %all-reduce.28.cloned.1.call-start = ((), (), s32[]{:S(2)}) async-start(), calls=%async_computation.13 | async-start | bytes 393216 | tf_op jit(solution)/shard_map/psum | solution.py:43
  7.8 3.8 copy-start.6
  7.8 4.0 copy-start.44
  7.8 4.0 copy-start.41
  7.9 4.4 copy-start.31
  7.9 4.4 copy-start.34
  7.9 10.6 %copy-start.47 = (s32[12]{0:T(128)S(1)}, s32[12]{0:T(128)}, u32[]{:S(2)}) copy-start(s32[12]{0:T(128)} %param.25) | copy-start | bytes 148
  10.8 55.7 %all-gather.6.cloned.1.call-start = ((), (), s32[]{:S(2)}) async-start(), calls=%async_computation.5 | async-start | bytes 2359296 | tf_op jit(solution)/shard_map/all_gather | solution.py:126
  11.5 112.7 %all-gather.8.cloned.1.call-start = ((), (), s32[]{:S(2)}) async-start(), calls=%async_computation.7 | async-start | bytes 2359296 | tf_op jit(solution)/shard_map/all_gather | solution.py:126
  11.8 52.8 %copy-start.32 = (f32[1,2,4,128]{3,1,2,0:T(2,128)}, f32[1,2,4,128]{3,1,2,0:T(2,128)S(1)}, u32[]{:S(2)}) copy-start(f32[1,2,4,128]{3,1,2,0:T(2,128)S(1)} %copy.245) | copy-start | bytes 12292
  64.5 1.0 copy-start.9
  69.4 2.5 copy-start.45
  71.1 87.1 %all-gather.4.cloned.1.call-start = ((), (), s32[]{:S(2)}) async-start(), calls=%async_computation.3 | async-start | bytes 5570560 | tf_op jit(solution)/shard_map/all_gather | solution.py:96
  71.6 100.7 %reduce-scatter.4.cloned.1.call-start = ((), (), s32[]{:S(2)}) async-start(), calls=%async_computation.4 | async-start | bytes 393216 | tf_op jit(solution)/shard_map/reduce_scatter | solution.py:100
  76.3 3.5 copy-start.52
  76.3 5.4 copy-start.50
  76.3 6.1 copy-start.49
  82.4 33.9 %copy-start.35 = (pred[8,64]{1,0:T(8,128)(4,1)}, pred[8,64]{1,0:T(8,128)(4,1)S(1)}, u32[]{:S(2)}) copy-start(pred[8,64]{1,0:T(8,128)(4,1)S(1)} %broadcast_compare_fusion) | copy-start | bytes 1540
  83.1 41.0 %copy-start.24 = (pred[12,8,4,4]{0,1,3,2:T(8,128)(4,1)}, pred[12,8,4,4]{0,1,3,2:T(8,128)(4,1)S(1)}, u32[]{:S(2)}) copy-start(pred[12,8,4,4]{0,1,3,2:T(8,128)(4,1)S(1)} %get-tuple-element.72) | copy-start | bytes 4612
  112.5 1.0 copy-start.14
  116.4 3.4 copy-start.1
  123.2 5.0 copy-start.15
  123.2 5.0 copy-start.39
  123.2 5.0 copy-start.40
  124.3 33.9 %copy-start.17 = (bf16[32,1280]{1,0:T(8,128)(2,1)S(1)}, bf16[32,1280]{1,0:T(8,128)(2,1)}, u32[]{:S(2)}) copy-start(bf16[32,1280]{1,0:T(8,128)(2,1)} %reshape.371) | copy-start | bytes 245764
  162.4 135.2 %reduce-scatter.6.cloned.1.call-start = ((), (), s32[]{:S(2)}) async-start(), calls=%async_computation.6 | async-start | bytes 835584 | tf_op jit(solution)/shard_map/reduce_scatter | solution.py:187
  164.5 2.9 copy-start.22
  164.5 7.9 %copy-start.46 = (f32[16]{0:T(128)S(1)}, f32[16]{0:T(128)}, u32[]{:S(2)}) copy-start(f32[16]{0:T(128)} %fusion.118) | copy-start | bytes 196
  166.6 7.1 %copy-start.33 = (f32[1,2,4,128]{3,1,2,0:T(2,128)S(1)}, f32[1,2,4,128]{3,1,2,0:T(2,128)}, u32[]{:S(2)}) copy-start(f32[1,2,4,128]{3,1,2,0:T(2,128)} %copy-done.32) | copy-start | bytes 12292
  167.5 6.4 %copy-start.42 = (pred[4,4]{1,0:T(4,128)(4,1)S(1)}, pred[4,4]{1,0:T(4,128)(4,1)}, u32[]{:S(2)}) copy-start(pred[4,4]{1,0:T(4,128)(4,1)} %broadcast_compare_fusion.1) | copy-start | bytes 52
  167.5 10.3 %copy-start.29 = (f32[8,8,4,2]{1,3,2,0:T(2,128)S(1)}, f32[8,8,4,2]{1,3,2,0:T(2,128)}, u32[]{:S(2)}) copy-start(f32[8,8,4,2]{1,3,2,0:T(2,128)} %get-tuple-element.78) | copy-start | bytes 6148
  167.5 10.4 %copy-start.28 = (f32[8,8,4,2]{1,3,2,0:T(2,128)S(1)}, f32[8,8,4,2]{1,3,2,0:T(2,128)}, u32[]{:S(2)}) copy-start(f32[8,8,4,2]{1,3,2,0:T(2,128)} %get-tuple-element.74) | copy-start | bytes 6148
  173.8 50.0 %copy-start.12 = (f32[8,8,4,2,64]{4,1,3,2,0:T(8,128)S(1)}, f32[8,8,4,2,64]{4,1,3,2,0:T(8,128)}, u32[]{:S(2)}) copy-start(f32[8,8,4,2,64]{4,1,3,2,0:T(8,128)} %get-tuple-element.79) | copy-start | bytes 393220
  221.5 3.9 copy-start.7
  225.4 2.1 copy-start.8
  225.4 2.4 copy-start.23
  226.8 2.3 copy-start.19
  226.8 3.2 copy-start.11
  226.8 116.6 %reduce-scatter.8.cloned.1.call-start = ((), (), s32[]{:S(2)}) async-start(), calls=%async_computation.8 | async-start | bytes 835584 | tf_op jit(solution)/shard_map/reduce_scatter | solution.py:187
  231.6 1.5 copy-start.48
  231.6 1.6 copy-start.51
  231.6 2.3 copy-start.30
  231.6 2.4 copy-start.18
  231.7 2.4 copy-start.25
  231.7 2.4 copy-start.43
  231.7 2.6 copy-start.13
  231.7 2.6 copy-start.27
  231.7 2.6 copy-start.36
  233.1 133.0 %copy-start.10 = (bf16[128,1280]{1,0:T(8,128)(2,1)S(1)}, bf16[128,1280]{1,0:T(8,128)(2,1)}, u32[]{:S(2)}) copy-start(bf16[128,1280]{1,0:T(8,128)(2,1)} %param.35) | copy-start | bytes 983044
  233.1 133.0 %all-reduce.24.cloned.1.call-start = ((), (), s32[]{:S(2)}) async-start(), calls=%async_computation.11 | async-start | bytes 198656 | tf_op jit(solution)/shard_map/psum | solution.py:190
  343.5 120.4 %all-reduce.22.cloned.1.call-start = ((), (), s32[]{:S(2)}) async-start(), calls=%async_computation.10 | async-start | bytes 1966080 | tf_op jit(solution)/shard_map/psum | solution.py:193
  367.9 103.3 %copy-start.37 = (f32[1280]{0:T(1024)S(1)}, f32[1280]{0:T(1024)}, u32[]{:S(2)}) copy-start(f32[1280]{0:T(1024)} %param.36) | copy-start | bytes 15364
  369.8 103.1 %copy-start.2 = (bf16[1280,640]{1,0:T(8,128)(2,1)S(1)}, bf16[1280,640]{1,0:T(8,128)(2,1)}, u32[]{:S(2)}) copy-start(bf16[1280,640]{1,0:T(8,128)(2,1)} %param.39) | copy-start | bytes 4915204
  369.8 103.1 %copy-start.26 = (f32[1280]{0:T(1024)S(1)}, f32[1280]{0:T(1024)}, u32[]{:S(2)}) copy-start(f32[1280]{0:T(1024)} %param.37) | copy-start | bytes 15364
  369.9 145.9 %all-reduce.26.cloned.1.call-start = ((), (), s32[]{:S(2)}) async-start(), calls=%async_computation.12 | async-start | bytes 1966080 | tf_op jit(solution)/shard_map/psum | solution.py:202
  471.2 2.9 copy-start.3
  472.9 2.2 copy-start.4
  476.2 1.2 copy-start.5
  477.4 135.4 %all-reduce.20.cloned.1.call-start = ((), (), s32[]{:S(2)}) async-start(), calls=%async_computation.9 | async-start | bytes 1966080 | tf_op jit(solution)/shard_map/psum | solution.py:209
  515.7 2.4 copy-start.20
  515.7 2.4 copy-start.21
  519.4 100.6 %copy-start.38 = (f32[1280]{0:T(1024)S(1)}, f32[1280]{0:T(1024)}, u32[]{:S(2)}) copy-start(f32[1280]{0:T(1024)} %param.41) | copy-start | bytes 15364
Sparse Core Ops, SparseCore 0:
  10.9 25.1 all-reduce.27
  37.6 27.1 all-gather.5
  71.2 25.6 all-gather.7
  98.9 59.2 all-gather.3
  162.5 9.8 reduce-scatter.3
  227.0 57.3 reduce-scatter.5
  287.9 55.5 reduce-scatter.7
  346.1 19.9 all-reduce.23
  370.0 93.8 all-reduce.21
  477.5 38.1 all-reduce.25
  519.6 93.1 all-reduce.19
where the time goes:
time: 630 us; the launch traced here: 629 us
  waiting for transfers between devices  340 us (54%)
  blocking collectives  167 us (27%)
  local copies, waits for them, and re-layouts  40.9 us (6%)
  matrix products  38.3 us (6%)
  other arithmetic  27.2 us (4%)
  between operations  14.9 us (2%)
    psum x1, waiting for transfers between devices, shards(): out_proj = lax.psum(partial_out, 'seq')  94 us
    psum x1, waiting for transfers between devices, shards(): lax.psum(jnp.dot(inner, w_down, preferred_element_type=f32), 'seq')  93.3 us
    unnamed x1, blocking collectives  60.1 us
    reduce_scatter x2, waiting for transfers between devices, shards(): lax.psum_scatter(weighted, 'seq', scatter_dimension=1, tiled=True)  45.9 us
    pmax x1, blocking collectives, shards(): top = lax.pmax(top, ('seq', 'head'))  40.8 us
    psum x1, waiting for transfers between devices, shards(): lax.psum((gate_part, up_part, jnp.sum(state_f * state_f, -1)), 'head')  33.1 us
    all_gather x1, waiting for transfers between devices, shards(): lax.all_gather(w_keyval, 'seq', axis=1, tiled=True)  28 us
    all_gather x1, blocking collectives, project_tokens(): lax.all_gather(kv_raw, 'seq', axis=1, tiled=True)  23.5 us
  transfers between devices with their start and end apart: 11, of which 8 were waited for; matrix products, arithmetic and copies ran while one was open for 9% of the time, Pallas kernels for 0%

commit v1 on v0

--- a/solution.py
+++ b/solution.py
@@ -44,10 +44,10 @@
     factor = lax.rsqrt(squares / D + EPS)[:, None]
     q_raw = (q_part * factor).astype(jnp.bfloat16)
     kv_raw = (kv_part * factor).astype(jnp.bfloat16)
-    q_raw, kv_raw = (
-        lax.all_gather(q_raw, "seq", axis=1, tiled=True),
-        lax.all_gather(kv_raw, "seq", axis=1, tiled=True),
-    )
+    block = q_raw.shape[1]
+    both = lax.all_gather(jnp.concatenate([q_raw, kv_raw], 1), "seq", axis=1)
+    q_raw = both[:, :, :block].reshape(both.shape[0], -1)
+    kv_raw = both[:, :, block:].reshape(both.shape[0], -1)
     queries = norm_heads(q_raw.astype(jnp.float32), q_gain, QSCALE).astype(jnp.bfloat16)
     fresh = finish_keys(kv_raw.astype(jnp.float32), k_gain)
     return (queries, fresh)
@@ -85,9 +85,6 @@
     steps, groups, beams, width = step_tokens.shape
     pre = prompt_states.shape[0]
     repeat = QH // KVH
-    col_block = QD // n_seq
-    block_head = jnp.arange(n_seq) * col_block // HD
-    head_pick = (jnp.arange(QH)[:, None] == block_head[None, :]).astype(f32)
     rows = jnp.transpose(prompt_states, (1, 0, 2)).astype(f32)
     prompt_scaled = (rows * in_gain).astype(bf16).reshape(-1, width)
     prompt_squares = jnp.sum(rows * rows, -1).reshape(-1)
@@ -110,7 +107,6 @@
     cache_ok = (flat_at * cache_seg + jnp.arange(cache_seg))[None, :] < cache_len[:, None]
     tail_seg = tail_cache.shape[2]
     local_beams = tail_cache.shape[1]
-    beam_ids = head_at * local_beams + jnp.arange(local_beams)
     offset = (seq_at * tail_seg + jnp.arange(tail_seg))[None, :] - tail_len[:, None]
     all_beams = jnp.arange(beams)
     every_query, every_fresh = project_tokens(
@@ -118,21 +114,30 @@
     )
     every_query = every_query.reshape(steps, groups, beams, -1)
     every_fresh = every_fresh.reshape(steps, groups, beams, -1)
-    tail_state = tail_cache
-    decoded = []
+    everyone = lax.all_gather(tail_cache, "head", axis=1, tiled=True)
+    local_ids = head_at * local_beams + jnp.arange(local_beams)
+    n_dev = n_seq * n_head
+    owner = jnp.broadcast_to(all_beams[None, :, None], (groups, beams, tail_seg))
+    source = jnp.broadcast_to(all_beams[None, :], (groups, beams))
+    ancestors = []
+    shaped_all, scores_all, tails_all = [], [], []
     for step in range(steps):
-        query = every_query[step]
-        new_pairs = every_fresh[step]
-        everyone = lax.all_gather(tail_state, "head", axis=1, tiled=True)
-        picks = lax.dynamic_slice_in_dim(parents[step], head_at * local_beams, local_beams, 1)
+        link = parents[step]
+        source = jnp.take_along_axis(source, link, axis=1)
+        ancestors = [jnp.take_along_axis(a, link, axis=1) for a in ancestors]
+        ancestors.append(jnp.broadcast_to(all_beams[None, :], (groups, beams)))
+        picks = lax.dynamic_slice_in_dim(source, head_at * local_beams, local_beams, 1)
         tail_state = jnp.take_along_axis(everyone, picks[:, :, None, None], axis=1)
-        owner = jnp.broadcast_to(all_beams[None, :, None], (groups, beams, tail_seg))
-        mine = lax.dynamic_slice_in_dim(new_pairs, head_at * local_beams, local_beams, 1)
-        tail_state = jnp.where((offset == step)[:, None, :, None], mine[:, :, None, :], tail_state)
+        for back, anc in enumerate(ancestors):
+            mine = lax.dynamic_slice_in_dim(anc, head_at * local_beams, local_beams, 1)
+            written = jnp.take_along_axis(every_fresh[back], mine[:, :, None], axis=1)
+            tail_state = jnp.where(
+                (offset == back)[:, None, :, None], written[:, :, None, :], tail_state
+            )
         tail_ok = (offset <= step)[:, None, None, :] & (
-            owner[:, :, None, :] == beam_ids[None, None, :, None]
-        )
-        shaped = query.reshape(groups, beams, KVH, repeat, HD)
+            owner[:, :, None, :] == local_ids[None, None, :, None]
+        )
+        shaped = every_query[step].reshape(groups, beams, KVH, repeat, HD)
         tail_keys, tail_values = split_pairs(tail_state)
         pre_scores = jnp.einsum(
             "gbkrd,gtkd->gbkrt", shaped[:pre], prompt_keys, preferred_element_type=f32
@@ -143,15 +148,23 @@
         tail_scores = jnp.einsum(
             "gbkrd,gctkd->gbkrct", shaped, tail_keys, preferred_element_type=f32
         )
+        pre_scores = jnp.where(prompt_ok[:, None, None, None, :], pre_scores, NEG)
+        dec_scores = jnp.where(cache_ok[:, None, None, None, :], dec_scores, NEG)
+        tail_scores = jnp.where(tail_ok[:, :, None, None, :, :], tail_scores, NEG)
+        top = jnp.concatenate([jnp.max(pre_scores, -1), jnp.max(dec_scores, -1)], 0)
+        top = jnp.maximum(top, jnp.max(tail_scores, (-2, -1)))
+        scores_all.append((pre_scores, dec_scores, tail_scores))
+        tails_all.append((tail_ok, tail_values))
+        shaped_all.append(top)
+    top_all = lax.pmax(jnp.stack(shaped_all), ("seq", "head"))
+    weighted_all, total_all = [], []
+    for step in range(steps):
+        pre_scores, dec_scores, tail_scores = scores_all[step]
+        tail_ok, tail_values = tails_all[step]
+        top = top_all[step]
         pre_mask = prompt_ok[:, None, None, None, :]
         dec_mask = cache_ok[:, None, None, None, :]
         tail_mask = tail_ok[:, :, None, None, :, :]
-        pre_scores = jnp.where(pre_mask, pre_scores, NEG)
-        dec_scores = jnp.where(dec_mask, dec_scores, NEG)
-        tail_scores = jnp.where(tail_mask, tail_scores, NEG)
-        top = jnp.concatenate([jnp.max(pre_scores, -1), jnp.max(dec_scores, -1)], 0)
-        top = jnp.maximum(top, jnp.max(tail_scores, (-2, -1)))
-        top = lax.pmax(top, ("seq", "head"))
         pre_weights = jnp.where(pre_mask, jnp.exp(pre_scores - top[:pre, ..., None]), 0.0)
         dec_weights = jnp.where(dec_mask, jnp.exp(dec_scores - top[pre:, ..., None]), 0.0)
         tail_weights = jnp.where(tail_mask, jnp.exp(tail_scores - top[..., None, None]), 0.0)
@@ -180,39 +193,57 @@
             tail_values,
             preferred_element_type=f32,
         )
-        weighted = weighted.reshape(groups * beams, -1)
-        total = total.reshape(groups * beams, -1)
-        spread_total = jnp.sum(total[:, :, None] * head_pick[None, :, :], 1)
-        share, own_total = (
-            lax.psum_scatter(weighted, "seq", scatter_dimension=1, tiled=True),
-            lax.psum_scatter(spread_total, "seq", scatter_dimension=1, tiled=True),
-        )
-        share, own_total = lax.psum((share, own_total), "head")
-        attn = (share / own_total).astype(bf16)
-        partial_out = jnp.dot(attn, w_out, preferred_element_type=f32)
-        out_proj = lax.psum(partial_out, "seq")
-        out_sq = lax.psum(jnp.sum(out_proj * out_proj, -1), "head")
-        x_f = step_tokens[step].reshape(groups * beams, -1).astype(f32)
-        state = (x_f + out_proj * lax.rsqrt(out_sq / D + EPS)[:, None] * post_gain).astype(bf16)
-        state = lax.optimization_barrier(state)
-        state_f = state.astype(f32)
-        scaled_two = (state_f * ffn_gain).astype(bf16)
-        gate_part = jnp.dot(scaled_two, w_gate, preferred_element_type=f32)
-        up_part = jnp.dot(scaled_two, w_up, preferred_element_type=f32)
-        gate_part, up_part, state_sq = lax.psum(
-            (gate_part, up_part, jnp.sum(state_f * state_f, -1)), "head"
-        )
-        norm_s = lax.rsqrt(state_sq / D + EPS)[:, None]
-        inner = (jax.nn.gelu(gate_part * norm_s, approximate=True) * (up_part * norm_s)).astype(
-            bf16
-        )
-        ffn_out = lax.psum(jnp.dot(inner, w_down, preferred_element_type=f32), "seq")
-        ffn_sq = lax.psum(jnp.sum(ffn_out * ffn_out, -1), "head")
-        result = (state_f + ffn_out * lax.rsqrt(ffn_sq / D + EPS)[:, None] * final_gain).astype(
-            bf16
-        )
-        decoded.append(result.reshape(groups, beams, -1))
-    return jnp.stack(decoded)
+        weighted_all.append(weighted.reshape(groups * beams, -1))
+        total_all.append(total.reshape(groups * beams, -1))
+    weighted = jnp.concatenate(weighted_all, 0)
+    total = jnp.concatenate(total_all, 0)
+    rows = weighted.shape[0]
+    piece = QD // n_seq
+    piece_head = jnp.arange(n_seq) * piece // HD
+    lanes = -(-rows // 128) * 128
+    packed = jnp.concatenate(
+        [
+            jnp.transpose(weighted.reshape(rows, n_seq, piece), (1, 0, 2)).reshape(n_seq, -1),
+            jnp.pad(jnp.transpose(total[:, piece_head]), ((0, 0), (0, lanes - rows))),
+        ],
+        1,
+    )
+    packed = lax.psum_scatter(packed, "seq", scatter_dimension=0, tiled=True)
+    packed = lax.psum(packed, "head")
+    share = packed[0, : rows * piece].reshape(rows, piece)
+    own_total = packed[0, rows * piece : rows * piece + rows]
+    attn = (share / own_total[:, None]).astype(bf16)
+    partial_out = jnp.dot(attn, w_out, preferred_element_type=f32)
+    per_dev = rows // n_seq
+    out_proj = lax.psum_scatter(
+        partial_out.reshape(n_seq, per_dev, -1), "seq", scatter_dimension=0, tiled=True
+    )[0]
+    out_sq = lax.psum(jnp.sum(out_proj * out_proj, -1), "head")
+    x_all = step_tokens.reshape(rows, -1)
+    x_f = lax.dynamic_slice_in_dim(x_all, seq_at * per_dev, per_dev, 0).astype(f32)
+    state = (x_f + out_proj * lax.rsqrt(out_sq / D + EPS)[:, None] * post_gain).astype(bf16)
+    state_all = lax.all_gather(state, "seq", axis=0, tiled=True)
+    state_f = state_all.astype(f32)
+    scaled_two = (state_f * ffn_gain).astype(bf16)
+    gate_part = jnp.dot(scaled_two, w_gate, preferred_element_type=f32)
+    up_part = jnp.dot(scaled_two, w_up, preferred_element_type=f32)
+    gate_part, up_part, state_sq = lax.psum(
+        (gate_part, up_part, jnp.sum(state_f * state_f, -1)), "head"
+    )
+    norm_s = lax.rsqrt(state_sq / D + EPS)[:, None]
+    inner = (jax.nn.gelu(gate_part * norm_s, approximate=True) * (up_part * norm_s)).astype(bf16)
+    ffn_out = lax.psum_scatter(
+        jnp.dot(inner, w_down, preferred_element_type=f32).reshape(n_seq, per_dev, -1),
+        "seq",
+        scatter_dimension=0,
+        tiled=True,
+    )[0]
+    ffn_sq = lax.psum(jnp.sum(ffn_out * ffn_out, -1), "head")
+    result = (
+        state.astype(f32) + ffn_out * lax.rsqrt(ffn_sq / D + EPS)[:, None] * final_gain
+    ).astype(bf16)
+    result = lax.all_gather(result, "seq", axis=0, tiled=True)
+    return result.reshape(steps, groups, beams, -1)
 
 
 def solution(mesh):

time: 630 us -> 639 us (1.014)
  blocking collectives: 167 us -> 104 us
  waiting for transfers between devices: 340 us -> 387 us
  local copies, waits for them, and re-layouts: 40.9 us -> 66.5 us
    psum x3 -> x1, waiting for transfers between devices: 210 us -> 20.5 us  [shards(): packed = lax.psum(packed, 'head')]
    unnamed x11 -> x12, waiting for transfers between devices: 1.37 us -> 190 us
    unnamed x1 -> x0, blocking collectives: 60.1 us -> none
    all_gather x2, waiting for transfers between devices: 0.03 us -> 41.1 us  [the longest x1 34.7 us: project_tokens(): both = lax.all_gather(jnp.concatenate([q_raw, kv_raw], 1), 'seq', axis=1)]
    reduce_scatter x2 -> x1, waiting for transfers between devices: 45.9 us -> 59.1 us  [shards(): lax.psum_scatter(jnp.dot(inner, w_down, preferred_element_type=f32).resha...]
    gather x0 -> x24, local copies, waits for them, and re-layouts: none -> 10.4 us  [the longest x10 5.3 us: shards(): written = jnp.take_along_axis(every_fresh[back], mine[:, :, None], axis=1)]
    all_gather x1, waiting for transfers between devices: 28 us -> 20.5 us  [shards(): lax.all_gather(w_keyval, 'seq', axis=1, tiled=True)]
  transfers between devices with their start and end apart: 11 -> 10, of which waited for: 8 -> 10; matrix products, arithmetic and copies ran while one was open for 9% -> 11% of each run, Pallas kernels for 0% -> 0%
where the time goes in v1:
time: 639 us; the launch traced here: 638 us
  waiting for transfers between devices  387 us (61%)
  blocking collectives  104 us (16%)
  local copies, waits for them, and re-layouts  66.5 us (10%)
  matrix products  35 us (5%)
  other arithmetic  30 us (5%)
  between operations  15.2 us (2%)
    unnamed x12, waiting for transfers between devices  190 us
    reduce_scatter x1, waiting for transfers between devices, shards(): lax.psum_scatter(jnp.dot(inner, w_down, preferred_element_type=f32).resha...  59.1 us
    pmax x1, blocking collectives, shards(): top_all = lax.pmax(jnp.stack(shaped_all), ('seq', 'head'))  40.5 us
    all_gather x1, waiting for transfers between devices, project_tokens(): both = lax.all_gather(jnp.concatenate([q_raw, kv_raw], 1), 'seq', axis=1)  34.7 us
    psum x1, waiting for transfers between devices, shards(): lax.psum((gate_part, up_part, jnp.sum(state_f * state_f, -1)), 'head')  31.1 us
    all_gather x1, blocking collectives, shards(): result = lax.all_gather(result, 'seq', axis=0, tiled=True)  21.3 us
    all_gather x1, blocking collectives, shards(): state_all = lax.all_gather(state, 'seq', axis=0, tiled=True)  21.2 us
    all_gather x1, waiting for transfers between devices, shards(): lax.all_gather(w_keyval, 'seq', axis=1, tiled=True)  20.5 us
  transfers between devices with their start and end apart: 10, of which 10 were waited for; matrix products, arithmetic and copies ran while one was open for 11% of the time, Pallas kernels for 0%

profile of v1, /device:TPU:0, one launch (start us, length us, event | category | flops | bytes accessed | tf_op | source)
XLA Modules:
  0.0 637.6 jit_solution(13518079163312761268)
XLA Ops:
  6.6 2.2 fusion.28
  8.8 2.1 fusion.27
  12.3 5.8 all-reduce.4
  18.1 18.1 %all-reduce.21.cloned.1.call-done = (f32[192,128]{1,0:T(8,128)}, f32[192,128]{1,0:T(8,128)}) async-done(((f32[192,128]{1,0:T(8,128)}, f32[192,128]{1,0:T(8,128)}), (f32[192,128]{1,0:T(8,128)}, f32[192,128]{1,0:T(8,128)})) %all-reduce.21.cloned.1.call-update) | async-done | bytes 196624 | tf_op jit(solution)/shard_map/psum | solution.py:43
  39.7 1.3 gather_fusion.2
  41.3 1.3 gather_fusion.5
  47.3 2.7 fusion.110
  50.0 2.6 reshape.490
  52.7 1.6 reshape.487
  58.6 6.4 %all-gather.9.cloned.1.call-done = bf16[12,8,4,2048]{3,2,1,0:T(4,128)(2,1)} async-done(((bf16[12,4,4,2048]{3,2,1,0:T(4,128)(2,1)}), bf16[12,8,4,2048]{3,2,1,0:T(4,128)(2,1)}) %all-gather.9.cloned.1.call-update) | async-done | bytes 1572880 | tf_op jit(solution)/shard_map/all_gather | solution.py:117
  65.0 4.0 gather_fusion.8
  69.0 2.5 gather_fusion.3
  71.5 34.7 %all-gather.11.cloned.1.call-done = bf16[192,4096]{1,0:T(8,128)(2,1)} async-done(((bf16[192,256]{1,0:T(8,128)(2,1)}), bf16[192,4096]{1,0:T(8,128)(2,1)}) %all-gather.11.cloned.1.call-update) | async-done | bytes 1572880 | tf_op jit(solution)/shard_map/all_gather | solution.py:48
  106.2 1.8 copy.317
  108.8 1.4 fusion.111
  112.1 1.5 mul.295
  115.2 1.6 gather_fusion.4
  116.9 1.6 gather_fusion.1
  118.5 1.6 gather_fusion.6
  122.1 2.4 select_select_fusion.1
  124.6 1.2 fusion.112
  126.7 1.2 fusion.113
  133.3 1.7 copy.241
  135.0 3.0 fusion.38
  138.0 2.8 copy.257
  140.8 1.7 fusion.17
  142.6 1.7 fusion.118
  144.3 1.7 fusion.120
  146.0 20.5 %all-gather.7.cloned.1.call-done = bf16[1280,2048]{1,0:T(8,128)(2,1)} async-done(((bf16[1280,128]{1,0:T(8,128)(2,1)}), bf16[1280,2048]{1,0:T(8,128)(2,1)}) %all-gather.7.cloned.1.call-update) | async-done | bytes 5242896 | tf_op jit(solution)/shard_map/all_gather | solution.py:93
  166.6 4.2 fusion.122
  171.9 1.1 reshape.492
  174.6 6.2 reduce-scatter.4.cloned.1.call-done
  182.3 1.3 fusion.121
  185.6 40.5 %pmax.7 = f32[2,12,8,4,2]{2,4,3,1,0:T(2,128)S(1)} all-reduce(f32[2,12,8,4,2]{2,4,3,1,0:T(2,128)S(1)} %pad_maximum_fusion.2), channel_id=1, replica_groups=mesh['seq'=16,'head'=2] {'seq','head'}, use_global_device_ids=true, to_apply=%region_17.21 | all-reduce | flops 1536 | bytes 12288 | tf_op jit(solution)/shard_map/pmax | solution.py:159
  227.7 1.4 fusion.79
  229.1 1.7 convolution_bitcast_fusion.5
  230.8 2.3 convolution_bitcast_fusion.2
  233.6 1.1 convolution_bitcast_fusion.3
  235.5 1.6 fusion.30
  240.7 1.1 copy.269
  241.9 1.9 copy.263
  243.7 1.5 fusion.3
  246.3 1.8 fusion.4
  248.5 1.5 concatenate.82
  250.8 1.2 copy_bitcast_fusion
  252.1 1.3 select_maximum_fusion
  254.6 94.9 %all-reduce.15.cloned.1.call-done = f32[16,24832]{1,0:T(8,128)} async-done(((f32[16,24832]{1,0:T(8,128)}), f32[16,24832]{1,0:T(8,128)}) %all-reduce.15.cloned.1.call-update) | async-done | bytes 1589264
  349.5 2.4 constant_dynamic-slice_fusion.2
  352.0 20.5 %all-reduce.13.cloned.1.call-done = f32[1,24832]{1,0:T(1,128)} async-done(((f32[1,24832]{1,0:T(1,128)}), f32[1,24832]{1,0:T(1,128)}) %all-reduce.13.cloned.1.call-update) | async-done | bytes 99344 | tf_op jit(solution)/shard_map/psum | solution.py:212
  373.2 1.1 slice_reduce_fusion
  374.5 1.3 fusion.42
  375.9 94.0 %all-reduce.17.cloned.1.call-done = f32[16,12,1280]{2,0,1:T(8,128)} async-done(((f32[16,12,1280]{2,0,1:T(8,128)}), f32[16,12,1280]{2,0,1:T(8,128)}) %all-reduce.17.cloned.1.call-update) | async-done | bytes 983056
  469.9 1.6 constant_dynamic-slice_fusion.1
  471.7 4.9 psum.67
  477.5 21.2 %all-gather.1 = bf16[16,12,1280]{2,1,0:T(8,128)(2,1)S(1)} all-gather(bf16[1,12,1280]{2,1,0:T(8,128)(2,1)S(1)} %fusion.108), channel_id=1, replica_groups=mesh['seq'=16,'head'=2] {'seq'}, dimensions={0}, use_global_device_ids=true | all-gather | bytes 522240 | tf_op jit(solution)/shard_map/all_gather | solution.py:225
  498.8 2.9 fusion.55
  501.7 1.4 fusion.56
  503.3 4.9 psum.69
  508.3 31.1 %all-reduce.19.cloned.1.call-done = (f32[192,640]{1,0:T(8,128)}, f32[192,640]{1,0:T(8,128)}) async-done(((f32[192,640]{1,0:T(8,128)}, f32[192,640]{1,0:T(8,128)}), (f32[192,640]{1,0:T(8,128)}, f32[192,640]{1,0:T(8,128)})) %all-reduce.19.cloned.1.call-update) | async-done | bytes 983056 | tf_op jit(solution)/shard_map/psum | solution.py:230
  539.4 1.9 fusion.44
  541.3 1.2 reshape.494
  542.5 59.1 %reduce-scatter.6.cloned.1.call-done = f32[1,12,1280]{2,1,0:T(8,128)} async-done(((f32[16,12,1280]{2,1,0:T(8,128)}), f32[1,12,1280]{2,1,0:T(8,128)}) %reduce-scatter.6.cloned.1.call-update) | async-done | bytes 61456 | tf_op jit(solution)/shard_map/reduce_scatter | solution.py:235
  602.6 4.9 psum.71
  608.6 21.3 %all-gather.2 = bf16[16,12,1280]{2,1,0:T(8,128)(2,1)S(1)} all-gather(bf16[1,12,1280]{2,1,0:T(8,128)(2,1)S(1)} %fusion.83), channel_id=1, replica_groups=mesh['seq'=16,'head'=2] {'seq'}, dimensions={0}, use_global_device_ids=true | all-gather | bytes 522240 | tf_op jit(solution)/shard_map/all_gather | solution.py:245
  (271 shorter events, 47.3 us)
Async XLA Ops:
  6.5 532.8 %copy-start = (bf16[640,1280]{1,0:T(8,128)(2,1)S(1)}, bf16[640,1280]{1,0:T(8,128)(2,1)}, u32[]{:S(2)}) copy-start(bf16[640,1280]{1,0:T(8,128)(2,1)} %param.44) | copy-start | bytes 4915204
  6.5 5.1 copy-start.17
  6.5 29.7 %all-reduce.21.cloned.1.call-start = ((), (), s32[]{:S(2)}) async-start(), calls=%async_computation.11 | async-start | bytes 393216 | tf_op jit(solution)/shard_map/psum | solution.py:43
  6.5 5.4 copy-start.30
  6.5 5.4 copy-start.39
  10.8 27.7 %copy-start.42 = (f32[256]{0:T(256)S(1)}, f32[256]{0:T(256)}, u32[]{:S(2)}) copy-start(f32[256]{0:T(256)} %param.38) | copy-start | bytes 3076
  10.8 27.8 %copy-start.45 = (s32[12]{0:T(128)S(1)}, s32[12]{0:T(128)}, u32[]{:S(2)}) copy-start(s32[12]{0:T(128)} %param.29) | copy-start | bytes 148
  10.9 28.6 %copy-start.43 = (f32[256]{0:T(256)S(1)}, f32[256]{0:T(256)}, u32[]{:S(2)}) copy-start(f32[256]{0:T(256)} %param.37) | copy-start | bytes 3076
  10.9 28.7 %copy-start.34 = (s32[2,12,8]{1,2,0:T(8,128)S(1)}, s32[2,12,8]{1,2,0:T(8,128)}, u32[]{:S(2)}) copy-start(s32[2,12,8]{1,2,0:T(8,128)} %param.27) | copy-start | bytes 2308
  10.9 54.1 %all-gather.9.cloned.1.call-start = ((), (), s32[]{:S(2)}) async-start(), calls=%async_computation.4 | async-start | bytes 2359296 | tf_op jit(solution)/shard_map/all_gather | solution.py:117
  11.6 94.5 %all-gather.11.cloned.1.call-start = ((), (), s32[]{:S(2)}) async-start(), calls=%async_computation.7 | async-start | bytes 1671168 | tf_op jit(solution)/shard_map/all_gather | solution.py:48
  37.9 128.7 %all-gather.7.cloned.1.call-start = ((), (), s32[]{:S(2)}) async-start(), calls=%async_computation.2 | async-start | bytes 5570560 | tf_op jit(solution)/shard_map/all_gather | solution.py:93
  38.5 142.3 %reduce-scatter.4.cloned.1.call-start = ((), (), s32[]{:S(2)}) async-start(), calls=%async_computation.3 | async-start | bytes 393216 | tf_op jit(solution)/shard_map/reduce_scatter | solution.py:97
  38.6 75.7 %copy-start.31 = (f32[1,2,4,128]{3,1,2,0:T(2,128)}, f32[1,2,4,128]{3,1,2,0:T(2,128)S(1)}, u32[]{:S(2)}) copy-start(f32[1,2,4,128]{3,1,2,0:T(2,128)S(1)} %copy.316) | copy-start | bytes 12292
  52.7 1.6 copy-start.49
  52.7 4.0 copy-start.47
  52.7 4.6 copy-start.46
  58.6 82.2 %copy-start.23 = (pred[12,8,4,4]{0,1,3,2:T(8,128)(4,1)}, pred[12,8,4,4]{0,1,3,2:T(8,128)(4,1)S(1)}, u32[]{:S(2)}) copy-start(pred[12,8,4,4]{0,1,3,2:T(8,128)(4,1)S(1)} %get-tuple-element.66) | copy-start | bytes 4612
  65.0 4.0 copy-start.9
  114.2 1.0 copy-start.11
  118.5 3.6 copy-start.5
  118.5 3.6 copy-start.38
  120.2 1.9 copy-start.6
  124.6 2.1 copy-start.7
  129.1 1.4 copy-start.2
  131.3 1.0 copy-start.18
  138.0 4.6 copy-start.1
  140.8 1.8 copy-start.36
  142.6 24.0 %copy-start.20 = (bf16[32,1280]{1,0:T(8,128)(2,1)S(1)}, bf16[32,1280]{1,0:T(8,128)(2,1)}, u32[]{:S(2)}) copy-start(bf16[32,1280]{1,0:T(8,128)(2,1)} %reshape.483) | copy-start | bytes 245764
  146.0 24.8 %copy-start.4 = (f32[12,4,4,4,8,2]{0,4,3,2,5,1:T(8,128)S(1)}, f32[12,4,4,4,8,2]{0,4,3,2,5,1:T(8,128)}, u32[]{:S(2)}) copy-start(f32[12,4,4,4,8,2]{0,4,3,2,5,1:T(8,128)} %copy.241) | copy-start | bytes 147460
  146.0 24.8 %copy-start.25 = (pred[12,8,4,4]{0,1,3,2:T(8,128)(4,1)S(1)}, pred[12,8,4,4]{0,1,3,2:T(8,128)(4,1)}, u32[]{:S(2)}) copy-start(pred[12,8,4,4]{0,1,3,2:T(8,128)(4,1)} %get-tuple-element.65) | copy-start | bytes 4612
  146.0 24.9 %copy-start.10 = (bf16[12,4,4,1024]{3,2,1,0:T(4,128)(2,1)S(1)}, bf16[12,4,4,1024]{3,2,1,0:T(4,128)(2,1)}, u32[]{:S(2)}) copy-start(bf16[12,4,4,1024]{3,2,1,0:T(4,128)(2,1)} %get-tuple-element.26) | copy-start | bytes 1179652
  170.8 2.3 copy-start.27
  170.8 10.0 %copy-start.44 = (f32[16]{0:T(128)S(1)}, f32[16]{0:T(128)}, u32[]{:S(2)}) copy-start(f32[16]{0:T(128)} %fusion.99) | copy-start | bytes 196
  170.8 178.7 %all-reduce.15.cloned.1.call-start = ((), (), s32[]{:S(2)}) async-start(), calls=%async_computation.8 | async-start | bytes 3178496
  170.9 11.2 %copy-start.32 = (f32[1,2,4,128]{3,1,2,0:T(2,128)S(1)}, f32[1,2,4,128]{3,1,2,0:T(2,128)}, u32[]{:S(2)}) copy-start(f32[1,2,4,128]{3,1,2,0:T(2,128)} %copy-done.31) | copy-start | bytes 12292
  171.9 10.4 %copy-start.41 = (pred[4,4]{1,0:T(4,128)(4,1)S(1)}, pred[4,4]{1,0:T(4,128)(4,1)}, u32[]{:S(2)}) copy-start(pred[4,4]{1,0:T(4,128)(4,1)} %broadcast_compare_fusion.1) | copy-start | bytes 52
  173.0 11.7 %copy-start.28 = (f32[8,8,4,2]{1,3,2,0:T(2,128)S(1)}, f32[8,8,4,2]{1,3,2,0:T(2,128)}, u32[]{:S(2)}) copy-start(f32[8,8,4,2]{1,3,2,0:T(2,128)} %get-tuple-element.67) | copy-start | bytes 6148
  174.6 9.0 %copy-start.29 = (bf16[32,2048]{1,0:T(8,128)(2,1)S(1)}, bf16[32,2048]{1,0:T(8,128)(2,1)}, u32[]{:S(2)}) copy-start(bf16[32,2048]{1,0:T(8,128)(2,1)} %get-tuple-element.33) | copy-start | bytes 393220
  174.6 10.1 %copy-start.21 = (f32[12,8,4,2]{1,3,2,0:T(2,128)S(1)}, f32[12,8,4,2]{1,3,2,0:T(2,128)}, u32[]{:S(2)}) copy-start(f32[12,8,4,2]{1,3,2,0:T(2,128)} %copy.258) | copy-start | bytes 9220
  182.1 48.6 %copy-start.14 = (f32[8,8,4,2,64]{4,1,3,2,0:T(8,128)S(1)}, f32[8,8,4,2,64]{4,1,3,2,0:T(8,128)}, u32[]{:S(2)}) copy-start(f32[8,8,4,2,64]{4,1,3,2,0:T(8,128)} %get-tuple-element.68) | copy-start | bytes 393220
  226.8 6.4 %copy-start.15 = (f32[8,8,4,2,64]{4,1,3,2,0:T(8,128)S(1)}, f32[8,8,4,2,64]{4,1,3,2,0:T(8,128)}, u32[]{:S(2)}) copy-start(f32[8,8,4,2,64]{4,1,3,2,0:T(8,128)} %get-tuple-element.72) | copy-start | bytes 393220
  226.8 6.4 %copy-start.37 = (pred[8,64]{1,0:T(8,128)(4,1)S(1)}, pred[8,64]{1,0:T(8,128)(4,1)}, u32[]{:S(2)}) copy-start(pred[8,64]{1,0:T(8,128)(4,1)} %broadcast_compare_fusion) | copy-start | bytes 1540
  229.1 4.5 copy-start.13
  233.1 1.6 copy-start.22
  233.1 2.4 copy-start.26
  233.6 4.2 copy-start.3
  233.6 4.2 copy-start.24
  237.1 4.8 copy-start.16
  245.3 1.1 copy-start.12
  253.3 0.7 copy-start.48
  253.3 121.2 %copy-start.19 = (bf16[128,1280]{1,0:T(8,128)(2,1)S(1)}, bf16[128,1280]{1,0:T(8,128)(2,1)}, u32[]{:S(2)}) copy-start(bf16[128,1280]{1,0:T(8,128)(2,1)} %param.39) | copy-start | bytes 983044
  253.4 119.1 %all-reduce.13.cloned.1.call-start = ((), (), s32[]{:S(2)}) async-start(), calls=%async_computation.5 | async-start | bytes 198656 | tf_op jit(solution)/shard_map/psum | solution.py:212
  351.9 118.0 %all-reduce.17.cloned.1.call-start = ((), (), s32[]{:S(2)}) async-start(), calls=%async_computation.9 | async-start | bytes 1966080
  373.2 103.4 %copy-start.35 = (f32[1280]{0:T(1024)S(1)}, f32[1280]{0:T(1024)}, u32[]{:S(2)}) copy-start(f32[1280]{0:T(1024)} %param.40) | copy-start | bytes 15364
  375.8 123.0 %copy-start.33 = (f32[1280]{0:T(1024)S(1)}, f32[1280]{0:T(1024)}, u32[]{:S(2)}) copy-start(f32[1280]{0:T(1024)} %param.41) | copy-start | bytes 15364
  375.8 163.5 %all-reduce.19.cloned.1.call-start = ((), (), s32[]{:S(2)}) async-start(), calls=%async_computation.10 | async-start | bytes 1966080 | tf_op jit(solution)/shard_map/psum | solution.py:230
  498.8 2.9 copy-start.8
  503.1 98.5 %reduce-scatter.6.cloned.1.call-start = ((), (), s32[]{:S(2)}) async-start(), calls=%async_computation.6 | async-start | bytes 1392640 | tf_op jit(solution)/shard_map/reduce_scatter | solution.py:235
  541.3 66.3 %copy-start.40 = (f32[1280]{0:T(1024)S(1)}, f32[1280]{0:T(1024)}, u32[]{:S(2)}) copy-start(f32[1280]{0:T(1024)} %param.45) | copy-start | bytes 15364
Sparse Core Ops, SparseCore 0:
  11.0 25.1 all-reduce.20
  37.7 27.1 all-gather.8
  67.2 38.9 all-gather.10
  108.2 58.3 all-gather.6
  170.9 9.8 reduce-scatter.3
  253.5 95.9 all-reduce.14
  352.0 20.3 all-reduce.12
  375.9 93.9 all-reduce.16
  503.2 36.0 all-reduce.18
  543.3 58.2 reduce-scatter.5
